TPU v7x, 32 devices: a whole 2x2x4 slice. The times are simulated.
32 devices in a mesh: pix: 16 (over z, y, x), mode: 2 (over core).
Axes of the slice: x: 2, y: 2, z: 4, core: 2. Of those that a mesh axis runs over, the one named last changes fastest.
Arguments:
- frames: float32 [384, 49152], P('mode', 'pix'), may hold values from -40 to 40
- basis: float32 [2048, 49152], P('mode', 'pix'), may hold values from -0.078125 to 0.078125
- annulus: int32 [64], P('pix'), may hold values from 0 to 7, as said below
- truncation: int32 [8], replicated, may hold values from 256 to 2048
Outputs:
- residual: float32 [384, 49152], P('mode', 'pix')
Inputs may be any that keep to these rules, and one draw needn't show every extreme that they name: Every annulus holds one block or more; the blocks of an annulus may lie anywhere in the image.
All inputs are finite; a program needn't handle non-finite values.
Results may differ from a plain program's by a relative error of at most 0.0001.
Values sent between devices are 32-bit elements; how exact they have to be, the bound alone decides.
No kernel may reach another device: no remote copies, remote signals or barrier semaphores. Data moves between devices by JAX's collectives and lax.ppermute only.
A program may use at most 128 MiB of HBM per device.

v0:
```python
import jax
import jax.numpy as jnp
from jax import lax
from jax.sharding import PartitionSpec as P

NA = 8
K_CHUNKS = 2
HIGHEST_PRECISION = lax.Precision.HIGHEST
PRODUCT_PRECISION = lax.Precision.HIGH


def butterfly_sum(value, axes, size):
    step = 1
    while step < size:
        pairs = [(i, i ^ step) for i in range(size)]
        value = value + lax.ppermute(value, axes, pairs)
        step *= 2
    return value


def local(frames, basis, annulus, truncation):
    own_rows, pix_dev = frames.shape
    groups = lax.axis_size("mode")
    parts = lax.axis_size("pix")
    total_frames = own_rows * groups
    blocks = annulus.shape[0]
    block_len = pix_dev // blocks
    modes_dev = basis.shape[0]
    gathered = lax.all_gather(frames, "mode", axis=0, tiled=True)
    mode_index = lax.axis_index("mode")
    onehot = (annulus[:, None] == jnp.arange(NA, dtype=jnp.int32)[None, :]).astype(jnp.float32)
    own_block_sums = jnp.stack(
        [jnp.sum(frames[:, b * block_len : (b + 1) * block_len], axis=1) for b in range(blocks)],
        axis=0,
    )
    own_sums = jnp.einsum("ba,bf->af", onehot, own_block_sums, precision=HIGHEST_PRECISION)
    frame_slot = (mode_index * own_rows + jnp.arange(own_rows, dtype=jnp.int32))[
        :, None
    ] == jnp.arange(total_frames, dtype=jnp.int32)[None, :]
    local_sums = jnp.einsum(
        "af,fg->ag", own_sums, frame_slot.astype(jnp.float32), precision=HIGHEST_PRECISION
    )
    first_group = (mode_index == 0).astype(jnp.float32)
    local_counts = jnp.sum(onehot, axis=0) * (block_len * first_group)
    own_slot = (lax.axis_index("pix") * blocks + jnp.arange(blocks, dtype=jnp.int32))[
        :, None
    ] == jnp.arange(parts * blocks, dtype=jnp.int32)[None, :]
    local_table = (
        jnp.einsum("ba,bc->ac", onehot, own_slot.astype(jnp.float32), precision=HIGHEST_PRECISION)
        * first_group
    )
    packed = butterfly_sum(
        jnp.concatenate([local_sums, local_counts[:, None], local_table], axis=1),
        ("pix", "mode"),
        parts * groups,
    )
    annulus_totals = packed[:, :total_frames]
    pixel_counts = packed[:, total_frames]
    every_onehot = packed[:, total_frames + 1 :].T
    mode_ids = mode_index * modes_dev + jnp.arange(modes_dev, dtype=jnp.int32)
    retained = (mode_ids[None, :] < truncation[:, None]).astype(jnp.float32)
    annulus_means = annulus_totals / pixel_counts[:, None]
    block_means = jnp.einsum("ba,af->bf", onehot, annulus_means, precision=HIGHEST_PRECISION)
    chunk = modes_dev // K_CHUNKS
    same_annulus = jnp.einsum("ca,ba->cb", every_onehot, every_onehot, precision=HIGHEST_PRECISION)
    block_retained = jnp.einsum("ba,ak->bk", every_onehot, retained, precision=HIGHEST_PRECISION)
    rows_dev = total_frames // parts

    def piece_of(c, b):
        return lax.dynamic_slice(basis, (c * chunk, b * block_len), (chunk, block_len))

    def outbound(c):

        def body(b, per_block):
            mean = lax.dynamic_index_in_dim(block_means, b, 0, keepdims=False)
            centered = (
                lax.dynamic_slice_in_dim(gathered, b * block_len, block_len, 1) - mean[:, None]
            )
            product = jnp.dot(centered, piece_of(c, b).T, precision=PRODUCT_PRECISION)
            return lax.dynamic_update_index_in_dim(per_block, product, b, 0)

        per_block = lax.fori_loop(
            0, blocks, body, jnp.zeros((blocks, total_frames, chunk), jnp.float32)
        )
        return per_block.reshape(blocks, parts, rows_dev, chunk).transpose(1, 0, 2, 3)

    def inbound(c, arrived):
        summed = jnp.einsum(
            "cb,bfk->cfk",
            same_annulus,
            arrived.reshape(parts * blocks, rows_dev, chunk),
            precision=HIGHEST_PRECISION,
        )
        outgoing = summed * block_retained[:, None, c * chunk : (c + 1) * chunk]
        return outgoing.reshape(parts, blocks, rows_dev, chunk)

    def model_of(c, returned):
        picked = returned.transpose(1, 0, 2, 3).reshape(blocks, total_frames, chunk)

        def body(b, term):
            coefficients = lax.dynamic_index_in_dim(picked, b, 0, keepdims=False)
            product = jnp.dot(coefficients, piece_of(c, b), precision=PRODUCT_PRECISION)
            return lax.dynamic_update_slice_in_dim(term, product, b * block_len, 1)

        return lax.fori_loop(0, blocks, body, jnp.zeros((total_frames, pix_dev), jnp.float32))

    term = None
    pending = None
    for stage in range(K_CHUNKS + 1):
        sending = []
        if stage < K_CHUNKS:
            sending.append(outbound(stage))
        if pending is not None:
            sending.append(pending)
        received = lax.all_to_all(jnp.stack(sending, axis=1), "pix", 0, 0, tiled=True)
        slot = 0
        next_pending = None
        if stage < K_CHUNKS:
            next_pending = inbound(stage, received[:, 0])
            slot = 1
        if pending is not None:
            part = model_of(stage - 1, received[:, slot])
            term = part if term is None else term + part
        pending = next_pending
    model_rows = lax.psum_scatter(term, "mode", scatter_dimension=0, tiled=True)
    own_means = lax.dynamic_slice_in_dim(block_means, mode_index * own_rows, own_rows, 1)
    own_centered = jnp.concatenate(
        [
            frames[:, b * block_len : (b + 1) * block_len] - own_means[b][:, None]
            for b in range(blocks)
        ],
        axis=1,
    )
    return own_centered - model_rows


def solution(mesh):
    return jax.shard_map(
        local,
        mesh=mesh,
        in_specs=(P("mode", "pix"), P("mode", "pix"), P("pix"), P()),
        out_specs=P("mode", "pix"),
        check_vma=False,
    )
```

profile of v0, /device:TPU:0, one launch (start us, length us, event | category | flops | bytes accessed | tf_op | source)
XLA Modules:
  0.0 523.1 jit_solution(12102426613418549742)
XLA Ops:
  30.1 78.8 %while.53 = (s32[]{:T(128)}, f32[4,384,512]{2,0,1:T(4,128)}, f32[384,3072]{1,0:T(8,128)}, f32[4,384]{1,0:T(4,128)S(1)}, f32[1024,3072]{1,0:T(8,128)}, /*index=5*/s32[]{:T(128)}, s32[]{:T(128)}, s32[]{:T(128)}, s32[]{:T(128)}) while((s32[]{:T(128)}, f32[4,384,512]{2,0,1:T(4,128)}, f32[384,3072]{1,0:T(8,128)}, f32[4,384]{1,0:T(4,128)S(1)}, ...), condition=%wide.region_8.9_spmd, body=%wide.region_7.8_spmd.sunk | while | flops 906264576 | bytes 6690451 | solution.py:82
  33.8 16.0 %dynamic_update_slice.36 = f32[4,384,512]{2,0,1:T(4,128)} dynamic-update-slice(f32[4,384,512]{2,0,1:T(4,128)} %get-tuple-element.572, f32[1,384,512]{2,0,1:T(1,128)S(1)} %copy.56, s32[]{:T(128)} %get-tuple-element.571, s32[]{:T(128)} %constant.181.clone.1..sunk.1, s32[]{:T(128)} %constant.181.clone.1..sunk.1) | dynamic-update-slice | bytes 1572868 | tf_op jit(solution)/shard_map/while/body/eval_jaxpr/jit(dynamic_update_index_in_dim)/dynamic_update_slice | solution.py:80
  53.5 16.0 %dynamic_update_slice.36 = f32[4,384,512]{2,0,1:T(4,128)} dynamic-update-slice(f32[4,384,512]{2,0,1:T(4,128)} %get-tuple-element.572, f32[1,384,512]{2,0,1:T(1,128)S(1)} %copy.56, s32[]{:T(128)} %get-tuple-element.571, s32[]{:T(128)} %constant.181.clone.1..sunk.1, s32[]{:T(128)} %constant.181.clone.1..sunk.1) | dynamic-update-slice | bytes 1572868 | tf_op jit(solution)/shard_map/while/body/eval_jaxpr/jit(dynamic_update_index_in_dim)/dynamic_update_slice | solution.py:80
  73.2 16.0 %dynamic_update_slice.36 = f32[4,384,512]{2,0,1:T(4,128)} dynamic-update-slice(f32[4,384,512]{2,0,1:T(4,128)} %get-tuple-element.572, f32[1,384,512]{2,0,1:T(1,128)S(1)} %copy.56, s32[]{:T(128)} %get-tuple-element.571, s32[]{:T(128)} %constant.181.clone.1..sunk.1, s32[]{:T(128)} %constant.181.clone.1..sunk.1) | dynamic-update-slice | bytes 1572868 | tf_op jit(solution)/shard_map/while/body/eval_jaxpr/jit(dynamic_update_index_in_dim)/dynamic_update_slice | solution.py:80
  92.9 16.0 %dynamic_update_slice.36 = f32[4,384,512]{2,0,1:T(4,128)} dynamic-update-slice(f32[4,384,512]{2,0,1:T(4,128)} %get-tuple-element.572, f32[1,384,512]{2,0,1:T(1,128)S(1)} %copy.56, s32[]{:T(128)} %get-tuple-element.571, s32[]{:T(128)} %constant.181.clone.1..sunk.1, s32[]{:T(128)} %constant.181.clone.1..sunk.1) | dynamic-update-slice | bytes 1572868 | tf_op jit(solution)/shard_map/while/body/eval_jaxpr/jit(dynamic_update_index_in_dim)/dynamic_update_slice | solution.py:80
  108.9 7.4 %all-to-all-start = ((f32[16,1,4,24,512]{4,2,3,1,0:T(4,128)}), f32[16,1,4,24,512]{4,2,3,1,0:T(4,128)}, u32[]{:S(2)}, u32[]{:S(2)}) async-start(f32[16,1,4,24,512]{4,2,3,1,0:T(4,128)} %bitcast.64), calls=%async_computation | async-start | bytes 6291456 | tf_op jit(solution)/shard_map/all_to_all | solution.py:115
  119.3 78.9 %while.52 = (s32[]{:T(128)}, f32[4,384,512]{2,0,1:T(4,128)}, f32[384,3072]{1,0:T(8,128)}, f32[4,384]{1,0:T(4,128)S(1)}, f32[1024,3072]{1,0:T(8,128)}, /*index=5*/s32[]{:T(128)}, s32[]{:T(128)}, s32[]{:T(128)}, s32[]{:T(128)}) while((s32[]{:T(128)}, f32[4,384,512]{2,0,1:T(4,128)}, f32[384,3072]{1,0:T(8,128)}, f32[4,384]{1,0:T(4,128)S(1)}, ...), condition=%wide.region_6.7_spmd, body=%wide.region_5.6_spmd.sunk | while | flops 906264576 | bytes 6690451 | solution.py:82
  123.0 16.0 %dynamic_update_slice.35 = f32[4,384,512]{2,0,1:T(4,128)} dynamic-update-slice(f32[4,384,512]{2,0,1:T(4,128)} %get-tuple-element.545, f32[1,384,512]{2,0,1:T(1,128)S(1)} %copy.55, s32[]{:T(128)} %get-tuple-element.544, s32[]{:T(128)} %constant.181.clone.1..sunk, s32[]{:T(128)} %constant.181.clone.1..sunk) | dynamic-update-slice | bytes 1572868 | tf_op jit(solution)/shard_map/while/body/eval_jaxpr/jit(dynamic_update_index_in_dim)/dynamic_update_slice | solution.py:80
  142.7 16.0 %dynamic_update_slice.35 = f32[4,384,512]{2,0,1:T(4,128)} dynamic-update-slice(f32[4,384,512]{2,0,1:T(4,128)} %get-tuple-element.545, f32[1,384,512]{2,0,1:T(1,128)S(1)} %copy.55, s32[]{:T(128)} %get-tuple-element.544, s32[]{:T(128)} %constant.181.clone.1..sunk, s32[]{:T(128)} %constant.181.clone.1..sunk) | dynamic-update-slice | bytes 1572868 | tf_op jit(solution)/shard_map/while/body/eval_jaxpr/jit(dynamic_update_index_in_dim)/dynamic_update_slice | solution.py:80
  162.4 16.0 %dynamic_update_slice.35 = f32[4,384,512]{2,0,1:T(4,128)} dynamic-update-slice(f32[4,384,512]{2,0,1:T(4,128)} %get-tuple-element.545, f32[1,384,512]{2,0,1:T(1,128)S(1)} %copy.55, s32[]{:T(128)} %get-tuple-element.544, s32[]{:T(128)} %constant.181.clone.1..sunk, s32[]{:T(128)} %constant.181.clone.1..sunk) | dynamic-update-slice | bytes 1572868 | tf_op jit(solution)/shard_map/while/body/eval_jaxpr/jit(dynamic_update_index_in_dim)/dynamic_update_slice | solution.py:80
  182.1 16.0 %dynamic_update_slice.35 = f32[4,384,512]{2,0,1:T(4,128)} dynamic-update-slice(f32[4,384,512]{2,0,1:T(4,128)} %get-tuple-element.545, f32[1,384,512]{2,0,1:T(1,128)S(1)} %copy.55, s32[]{:T(128)} %get-tuple-element.544, s32[]{:T(128)} %constant.181.clone.1..sunk, s32[]{:T(128)} %constant.181.clone.1..sunk) | dynamic-update-slice | bytes 1572868 | tf_op jit(solution)/shard_map/while/body/eval_jaxpr/jit(dynamic_update_index_in_dim)/dynamic_update_slice | solution.py:80
  198.1 4.5 copy.27
  202.6 4.9 reshape_squeeze.6
  207.5 6.3 %broadcast_multiply_fusion.1 = f32[64,24,512]{2,0,1:T(8,128)} fusion(f32[64,512]{1,0:T(8,128)S(1)} %get-tuple-element.418, f32[64,64,1]{1,0,2:T(8,128)S(1)} %convolution_bitcast_fusion, f32[64,24,512]{2,0,1:T(8,128)} %reshape_squeeze.6), kind=kOutput, calls=%fused_computation.32 | convolution fusion | flops 604766208 | bytes 6438912 | tf_op jit(solution)/shard_map/cb,bfk->cfk/dot_general | solution.py:88
  213.9 4.8 stack_reshape.6
  218.7 4.6 pad_maximum_fusion
  223.3 143.2 %all_to_all.15 = f32[16,2,4,24,512]{4,2,3,1,0:T(4,128)S(1)} all-to-all(f32[16,2,4,24,512]{4,2,3,1,0:T(4,128)S(1)} %pad_maximum_fusion), channel_id=1, replica_groups=mesh['pix'=16,'mode'=2] {'pix'}, dimensions={0} | all-to-all | bytes 12582912 | tf_op jit(solution)/shard_map/all_to_all | solution.py:115
  372.3 4.9 reshape_squeeze.7
  377.2 6.4 %broadcast_multiply_fusion = f32[64,24,512]{2,0,1:T(8,128)} fusion(f32[64,512]{1,0:T(8,128)S(1)} %get-tuple-element.417, f32[64,64,1]{1,0,2:T(8,128)S(1)} %convolution_bitcast_fusion, f32[64,24,512]{2,0,1:T(8,128)} %reshape_squeeze.7), kind=kOutput, calls=%fused_computation.31 | convolution fusion | flops 604766208 | bytes 6438912 | tf_op jit(solution)/shard_map/cb,bfk->cfk/dot_general | solution.py:88
  383.6 4.8 stack_reshape.7
  388.4 4.4 copy.31
  392.8 4.5 all-to-all-start.2
  400.2 24.9 %while.54 = (s32[]{:T(128)}, f32[384,3072]{1,0:T(8,128)}, f32[4,384,512]{2,0,1:T(4,128)}, f32[1024,3072]{1,0:T(8,128)}, s32[]{:T(128)}, /*index=5*/s32[]{:T(128)}, s32[]{:T(128)}, s32[]{:T(128)}) while((s32[]{:T(128)}, f32[384,3072]{1,0:T(8,128)}, f32[4,384,512]{2,0,1:T(4,128)}, f32[1024,3072]{1,0:T(8,128)}, s32[]{:T(128)}, ...), condition=%wide.region_10.11_spmd, body=%wide.region_9.10_spmd.sunk | while | flops 905969664 | bytes 5112967 | solution.py:105
  402.8 3.7 fusion.80
  415.2 3.6 fusion.80
  421.4 3.7 fusion.80
  425.1 31.7 %all-to-all-done.2 = f32[16,1,4,24,512]{4,2,3,1,0:T(4,128)} async-done(((f32[16,1,4,24,512]{4,2,3,1,0:T(4,128)}), f32[16,1,4,24,512]{4,2,3,1,0:T(4,128)}, u32[]{:S(2)}, u32[]{:S(2)}) %all-to-all-start.2) | async-done | bytes 3145760 | tf_op jit(solution)/shard_map/all_to_all | solution.py:115
  459.5 24.9 %while.55 = (s32[]{:T(128)}, f32[384,3072]{1,0:T(8,128)}, f32[4,384,512]{2,0,1:T(4,128)}, f32[1024,3072]{1,0:T(8,128)}, s32[]{:T(128)}, /*index=5*/s32[]{:T(128)}, s32[]{:T(128)}, s32[]{:T(128)}) while((s32[]{:T(128)}, f32[384,3072]{1,0:T(8,128)}, f32[4,384,512]{2,0,1:T(4,128)}, f32[1024,3072]{1,0:T(8,128)}, s32[]{:T(128)}, ...), condition=%wide.region_12.13_spmd, body=%wide.region_11.12_spmd.sunk | while | flops 905969664 | bytes 5112967 | solution.py:105
  462.1 3.7 fusion.82
  480.7 3.7 fusion.82
  484.5 6.9 %add.186 = f32[384,3072]{1,0:T(8,128)} add(f32[384,3072]{1,0:T(8,128)} %get-tuple-element.353, f32[384,3072]{1,0:T(8,128)} %get-tuple-element.354) | non-fusion elementwise | flops 1179648 | bytes 14155776 | tf_op jit(solution)/shard_map/add | solution.py:123
  492.7 19.9 %reduce-scatter.2.cloned.1.call-done = f32[192,3072]{1,0:T(8,128)} async-done(((f32[384,3072]{1,0:T(8,128)}), f32[192,3072]{1,0:T(8,128)}) %reduce-scatter.2.cloned.1.call-update) | async-done | bytes 2359312 | tf_op jit(solution)/shard_map/reduce_scatter | solution.py:125
  (87 shorter events, 103.9 us)
Async XLA Ops:
  6.5 1.7 copy-start
  6.5 1.9 copy-start.2
  6.5 21.4 %all-gather.2.cloned.1.call-start = ((), (), s32[]{:S(2)}) async-start(), calls=%async_computation.4 | async-start | bytes 7077888 | tf_op jit(solution)/shard_map/all_gather | solution.py:29
  9.3 1.3 collective-permute-start
  10.7 4.5 collective-permute-start.1
  15.2 3.8 collective-permute-start.2
  19.0 3.8 collective-permute-start.3
  22.8 4.8 collective-permute-start.4
  108.9 7.8 %copy-start.1 = (s32[8]{0:T(128)S(1)}, s32[8]{0:T(128)}, u32[]{:S(2)}) copy-start(s32[8]{0:T(128)} %param.15) | copy-start | bytes 100
  108.9 89.2 %all-to-all-start = ((f32[16,1,4,24,512]{4,2,3,1,0:T(4,128)}), f32[16,1,4,24,512]{4,2,3,1,0:T(4,128)}, u32[]{:S(2)}, u32[]{:S(2)}) async-start(f32[16,1,4,24,512]{4,2,3,1,0:T(4,128)} %bitcast.64), calls=%async_computation | async-start | bytes 6291456 | tf_op jit(solution)/shard_map/all_to_all | solution.py:115
  392.8 64.0 %all-to-all-start.2 = ((f32[16,1,4,24,512]{4,2,3,1,0:T(4,128)}), f32[16,1,4,24,512]{4,2,3,1,0:T(4,128)}, u32[]{:S(2)}, u32[]{:S(2)}) async-start(f32[16,1,4,24,512]{4,2,3,1,0:T(4,128)} %copy.31), calls=%async_computation.2 | async-start | bytes 6291456 | tf_op jit(solution)/shard_map/all_to_all | solution.py:115
  397.3 115.3 %reduce-scatter.2.cloned.1.call-start = ((), (), s32[]{:S(2)}) async-start(), calls=%async_computation.5 | async-start | bytes 7077888 | tf_op jit(solution)/shard_map/reduce_scatter | solution.py:125
Sparse Core Ops, SparseCore 0:
  8.9 17.1 all-gather.1
  491.5 21.0 reduce-scatter.1
where the time goes:
time: 528 us; the launch traced here: 523 us
  local copies, waits for them, and re-layouts  199 us (38%)
  blocking collectives  143 us (27%)
  matrix products  66.8 us (13%)
  waiting for transfers between devices  60.1 us (11%)
  starting transfers between devices  22.4 us (4%)
  other arithmetic  17.6 us (3%)
  between operations  13.5 us (3%)
    all_to_all x1, blocking collectives, local(): lax.all_to_all(jnp.stack(sending, axis=1), 'pix', 0, 0, tiled=True)  143 us
    dynamic_update_slice x16, local copies, waits for them, and re-layouts, body(): return lax.dynamic_update_index_in_dim(per_block, product, b, 0)  134 us
    all_to_all x2, waiting for transfers between devices, local(): lax.all_to_all(jnp.stack(sending, axis=1), 'pix', 0, 0, tiled=True)  31.7 us
    dot_general x8, matrix products, body(): product = jnp.dot(coefficients, piece_of(c, b), precision=PRODUCT_PRECISION)  29.3 us
    dot_general x8, matrix products, body(): product = jnp.dot(centered, piece_of(c, b).T, precision=PRODUCT_PRECISION)  23.1 us
    dynamic_slice x8, local copies, waits for them, and re-layouts, body(): coefficients = lax.dynamic_index_in_dim(picked, b, 0, keepdims=False)  20.5 us
    reduce_scatter x1, waiting for transfers between devices, local(): model_rows = lax.psum_scatter(term, 'mode', scatter_dimension=0, tiled=True)  19.9 us
    another operation x3, local copies, waits for them, and re-layouts, local(): jnp.stack(sending, axis=1)  14.1 us
  transfers between devices with their start and end apart: 9, of which 7 were waited for; matrix products, arithmetic and copies ran while one was open for 22% of the time, Pallas kernels for 0%

commit v1 on v0

--- a/solution.py
+++ b/solution.py
@@ -7,6 +7,22 @@
 K_CHUNKS = 2
 HIGHEST_PRECISION = lax.Precision.HIGHEST
 PRODUCT_PRECISION = lax.Precision.HIGH
+
+
+def exchange_in_pairs(x, axis, split, join):
+    ways, here = (lax.axis_size(axis), lax.axis_index(axis))
+    width = x.shape[split] // ways
+    shape = list(x.shape)
+    shape[split] = width
+    height = shape[join]
+    shape[join] = height * ways
+    full = jnp.zeros(shape, x.dtype)
+    for mask in range(ways):
+        part = lax.dynamic_slice_in_dim(x, (here ^ mask) * width, width, axis=split)
+        if mask:
+            part = lax.ppermute(part, axis, [(d, d ^ mask) for d in range(ways)])
+        full = lax.dynamic_update_slice_in_dim(full, part, (here ^ mask) * height, axis=join)
+    return full
 
 
 def butterfly_sum(value, axes, size):
@@ -112,7 +128,7 @@
             sending.append(outbound(stage))
         if pending is not None:
             sending.append(pending)
-        received = lax.all_to_all(jnp.stack(sending, axis=1), "pix", 0, 0, tiled=True)
+        received = exchange_in_pairs(jnp.stack(sending, axis=1), "pix", 0, 0)
         slot = 0
         next_pending = None
         if stage < K_CHUNKS:

time: 528 us -> 483 us (0.915)
  blocking collectives: 143 us -> 0 us
  starting transfers between devices: 22.4 us -> 150 us
  local copies, waits for them, and re-layouts: 199 us -> 73.2 us
  waiting for transfers between devices: 60.1 us -> 162 us
    all_to_all x1 -> x0, blocking collectives: 143 us -> none  [local(): lax.all_to_all(jnp.stack(sending, axis=1), 'pix', 0, 0, tiled=True)]
    ppermute x0 -> x45, starting transfers between devices: none -> 139 us  [exchange_in_pairs(): part = lax.ppermute(part, axis, [(d, d ^ mask) for d in range(ways)])]
    ppermute x0 -> x45, waiting for transfers between devices: none -> 137 us  [exchange_in_pairs(): part = lax.ppermute(part, axis, [(d, d ^ mask) for d in range(ways)])]
    dynamic_update_slice x16 -> x47, local copies, waits for them, and re-layouts: 134 us -> 25.5 us  [exchange_in_pairs(): lax.dynamic_update_slice_in_dim(full, part, (here ^ mask) * height, axis=...]
    all_to_all x2 -> x0, waiting for transfers between devices: 31.7 us -> none  [local(): lax.all_to_all(jnp.stack(sending, axis=1), 'pix', 0, 0, tiled=True)]
    dynamic_slice x8 -> x2, local copies, waits for them, and re-layouts: 20.5 us -> 3.57 us  [exchange_in_pairs(): part = lax.dynamic_slice_in_dim(x, (here ^ mask) * width, width, axis=split)]
    all_to_all x2 -> x0, starting transfers between devices: 11.9 us -> none  [local(): lax.all_to_all(jnp.stack(sending, axis=1), 'pix', 0, 0, tiled=True)]
    another operation x7, local copies, waits for them, and re-layouts: 23.9 us -> 16.8 us  [the longest x3 14.1 us: local(): jnp.stack(sending, axis=1)]
  transfers between devices with their start and end apart: 9 -> 52, of which waited for: 7 -> 21; matrix products, arithmetic and copies ran while one was open for 22% -> 15% of each run, Pallas kernels for 0% -> 0%
where the time goes in v1:
time: 483 us; the launch traced here: 481 us
  waiting for transfers between devices  162 us (34%)
  starting transfers between devices  150 us (31%)
  local copies, waits for them, and re-layouts  73.2 us (15%)
  matrix products  65 us (13%)
  other arithmetic  17.1 us (4%)
  between operations  14.1 us (3%)
    ppermute x45, starting transfers between devices, exchange_in_pairs(): part = lax.ppermute(part, axis, [(d, d ^ mask) for d in range(ways)])  139 us
    ppermute x45, waiting for transfers between devices, exchange_in_pairs(): part = lax.ppermute(part, axis, [(d, d ^ mask) for d in range(ways)])  137 us
    dot_general x8, matrix products, body(): product = jnp.dot(coefficients, piece_of(c, b), precision=PRODUCT_PRECISION)  29.3 us
    dynamic_update_slice x47, local copies, waits for them, and re-layouts, exchange_in_pairs(): lax.dynamic_update_slice_in_dim(full, part, (here ^ mask) * height, axis=...  25.5 us
    dot_general x8, matrix products, body(): product = jnp.dot(centered, piece_of(c, b).T, precision=PRODUCT_PRECISION)  23.1 us
    reduce_scatter x1, waiting for transfers between devices, local(): model_rows = lax.psum_scatter(term, 'mode', scatter_dimension=0, tiled=True)  17 us
    dot_general x2, matrix products, inbound(): jnp.einsum('cb,bfk->cfk', same_annulus, arrived.reshape(parts * blocks, r...  10.8 us
    ppermute x5, starting transfers between devices, butterfly_sum(): value = value + lax.ppermute(value, axes, pairs)  10.5 us
  transfers between devices with their start and end apart: 52, of which 21 were waited for; matrix products, arithmetic and copies ran while one was open for 15% of the time, Pallas kernels for 0%

profile of v1, /device:TPU:0, one launch (start us, length us, event | category | flops | bytes accessed | tf_op | source)
XLA Modules:
  0.0 481.2 jit_solution(9580562444360894323)
XLA Ops:
  29.7 11.8 %while.53 = (s32[]{:T(128)}, f32[4,384,512]{2,1,0:T(8,128)S(1)}, f32[384,3072]{1,0:T(8,128)}, f32[4,384]{1,0:T(4,128)S(1)}, f32[1024,3072]{1,0:T(8,128)}, /*index=5*/s32[]{:T(128)}, s32[]{:T(128)}, s32[]{:T(128)}, s32[]{:T(128)}) while((s32[]{:T(128)}, f32[4,384,512]{2,1,0:T(8,128)S(1)}, f32[384,3072]{1,0:T(8,128)}, f32[4,384]{1,0:T(4,128)S(1)}, ...), condition=%wide.region_8.9_spmd, body=%wide.region_7.8_spmd.sunk | while | flops 906264576 | bytes 3545743 | solution.py:98
  50.3 11.8 %while.52 = (s32[]{:T(128)}, f32[4,384,512]{2,1,0:T(8,128)S(1)}, f32[384,3072]{1,0:T(8,128)}, f32[4,384]{1,0:T(4,128)S(1)}, f32[1024,3072]{1,0:T(8,128)}, /*index=5*/s32[]{:T(128)}, s32[]{:T(128)}, s32[]{:T(128)}, s32[]{:T(128)}) while((s32[]{:T(128)}, f32[4,384,512]{2,1,0:T(8,128)S(1)}, f32[384,3072]{1,0:T(8,128)}, f32[4,384]{1,0:T(4,128)S(1)}, ...), condition=%wide.region_6.7_spmd, body=%wide.region_5.6_spmd.sunk | while | flops 906264576 | bytes 3545743 | solution.py:98
  63.7 3.9 copy.167
  91.0 3.9 collective-permute-start.16
  95.7 11.1 %collective-permute-done.12 = f32[1,1,4,24,512]{4,3,2,1,0:T(8,128)S(1)} collective-permute-done((f32[1,1,4,24,512]{4,3,2,1,0:T(8,128)S(1)}, f32[1,1,4,24,512]{4,3,2,1,0:T(8,128)S(1)}, u32[]{:S(2)}, u32[]{:S(2)}) %collective-permute-start.12) | collective-permute-done | bytes 196640 | tf_op jit(solution)/shard_map/ppermute | solution.py:23
  111.3 5.2 %collective-permute-done.13 = f32[1,1,4,24,512]{4,3,2,1,0:T(8,128)S(1)} collective-permute-done((f32[1,1,4,24,512]{4,3,2,1,0:T(8,128)S(1)}, f32[1,1,4,24,512]{4,3,2,1,0:T(8,128)S(1)}, u32[]{:S(2)}, u32[]{:S(2)}) %collective-permute-start.13) | collective-permute-done | bytes 196640 | tf_op jit(solution)/shard_map/ppermute | solution.py:23
  116.5 8.0 %collective-permute-start.18 = (f32[1,1,4,24,512]{4,3,2,1,0:T(8,128)S(1)}, f32[1,1,4,24,512]{4,3,2,1,0:T(8,128)S(1)}, u32[]{:S(2)}, u32[]{:S(2)}) collective-permute-start(f32[1,1,4,24,512]{4,3,2,1,0:T(8,128)S(1)} %copy-done.13), channel_id=1, source_target_pairs={{0,28},{2,30},{4,24},{6,26},{8,20},{10,22},{12,16},{14,18},{16,12}... | collective-permute-start | bytes 589832 | tf_op jit(solution)/shard_map/ppermute | solution.py:23
  125.3 4.5 collective-permute-start.19
  135.5 5.0 %reshape_squeeze.6 = f32[64,24,512]{2,0,1:T(8,128)} reshape(f32[16,1,4,24,512]{4,2,0,3,1:T(4,128)} %copy_dynamic-update-slice_fusion.15) | data formatting | bytes 6291456 | tf_op jit(solution)/shard_map/reshape;squeeze | solution.py:107
  140.5 6.3 %convolution_multiply_fusion.1 = f32[64,24,512]{2,0,1:T(8,128)} fusion(f32[64,64,1]{1,0,2:T(8,128)S(1)} %convolution_bitcast_fusion, f32[64,24,512]{2,0,1:T(8,128)} %reshape_squeeze.6, f32[64,512]{1,0:T(8,128)S(1)} %copy-done.8), kind=kOutput, calls=%fused_computation.68 | convolution fusion | flops 604766208 | bytes 6438912 | tf_op jit(solution)/shard_map/cb,bfk->cfk/dot_general | solution.py:104
  146.8 4.8 stack_reshape.6
  162.3 12.4 %collective-permute-start.23 = (f32[1,2,4,24,512]{4,2,0,3,1:T(4,128)}, f32[1,2,4,24,512]{4,2,0,3,1:T(4,128)S(1)}, u32[]{:S(2)}, u32[]{:S(2)}) collective-permute-start(f32[1,2,4,24,512]{4,2,0,3,1:T(4,128)} %get-tuple-element.402), channel_id=1, source_target_pairs={{0,8},{2,10},{4,12},{6,14},{8,0},{10,2},{12,4},{14,6},{16,24},{18,... | collective-permute-start | bytes 1179656 | tf_op jit(solution)/shard_map/ppermute | solution.py:23
  177.2 8.5 %collective-permute-start.25 = (f32[1,2,4,24,512]{4,2,0,3,1:T(4,128)S(1)}, f32[1,2,4,24,512]{4,2,0,3,1:T(4,128)S(1)}, u32[]{:S(2)}, u32[]{:S(2)}) collective-permute-start(f32[1,2,4,24,512]{4,2,0,3,1:T(4,128)S(1)} %get-tuple-element.405), channel_id=1, source_target_pairs={{0,12},{2,14},{4,8},{6,10},{8,4},{10,6},{12,0},{14,2},{16,28},{18,... | collective-permute-start | bytes 1179656 | tf_op jit(solution)/shard_map/ppermute | solution.py:23
  187.0 17.8 %collective-permute-start.27 = (f32[1,2,4,24,512]{4,2,0,3,1:T(4,128)S(1)}, f32[1,2,4,24,512]{4,2,0,3,1:T(4,128)S(1)}, u32[]{:S(2)}, u32[]{:S(2)}) collective-permute-start(f32[1,2,4,24,512]{4,2,0,3,1:T(4,128)S(1)} %get-tuple-element.407), channel_id=1, source_target_pairs={{0,16},{2,18},{4,20},{6,22},{8,24},{10,26},{12,28},{14,30},{16,0},... | collective-permute-start | bytes 1179656 | tf_op jit(solution)/shard_map/ppermute | solution.py:23
  207.9 7.3 %collective-permute-done.25 = f32[1,2,4,24,512]{4,2,0,3,1:T(4,128)S(1)} collective-permute-done((f32[1,2,4,24,512]{4,2,0,3,1:T(4,128)S(1)}, f32[1,2,4,24,512]{4,2,0,3,1:T(4,128)S(1)}, u32[]{:S(2)}, u32[]{:S(2)}) %collective-permute-start.25) | collective-permute-done | bytes 393248 | tf_op jit(solution)/shard_map/ppermute | solution.py:23
  216.5 4.2 collective-permute-done.26
  223.0 41.8 %collective-permute-done.27 = f32[1,2,4,24,512]{4,2,0,3,1:T(4,128)S(1)} collective-permute-done((f32[1,2,4,24,512]{4,2,0,3,1:T(4,128)S(1)}, f32[1,2,4,24,512]{4,2,0,3,1:T(4,128)S(1)}, u32[]{:S(2)}, u32[]{:S(2)}) %collective-permute-start.27) | collective-permute-done | bytes 393248 | tf_op jit(solution)/shard_map/ppermute | solution.py:23
  265.4 13.3 %collective-permute-done.28 = f32[1,2,4,24,512]{4,2,0,3,1:T(4,128)S(1)} collective-permute-done((f32[1,2,4,24,512]{4,2,0,3,1:T(4,128)S(1)}, f32[1,2,4,24,512]{4,2,0,3,1:T(4,128)S(1)}, u32[]{:S(2)}, u32[]{:S(2)}) %collective-permute-start.28) | collective-permute-done | bytes 393248 | tf_op jit(solution)/shard_map/ppermute | solution.py:23
  278.8 15.2 %collective-permute-done.29 = f32[1,2,4,24,512]{4,2,0,3,1:T(4,128)S(1)} collective-permute-done((f32[1,2,4,24,512]{4,2,0,3,1:T(4,128)S(1)}, f32[1,2,4,24,512]{4,2,0,3,1:T(4,128)S(1)}, u32[]{:S(2)}, u32[]{:S(2)}) %collective-permute-start.29) | collective-permute-done | bytes 393248 | tf_op jit(solution)/shard_map/ppermute | solution.py:23
  294.1 6.4 %collective-permute-done.30 = f32[1,2,4,24,512]{4,2,0,3,1:T(4,128)S(1)} collective-permute-done((f32[1,2,4,24,512]{4,2,0,3,1:T(4,128)S(1)}, f32[1,2,4,24,512]{4,2,0,3,1:T(4,128)S(1)}, u32[]{:S(2)}, u32[]{:S(2)}) %collective-permute-start.30) | collective-permute-done | bytes 393248 | tf_op jit(solution)/shard_map/ppermute | solution.py:23
  300.8 4.8 collective-permute-done.34
  312.5 4.5 convolution_multiply_fusion
  326.6 22.1 %collective-permute-start.38 = (f32[1,1,4,24,512]{4,2,0,3,1:T(4,128)}, f32[1,1,4,24,512]{4,2,0,3,1:T(4,128)}, u32[]{:S(2)}, u32[]{:S(2)}) collective-permute-start(f32[1,1,4,24,512]{4,2,0,3,1:T(4,128)} %get-tuple-element.424), channel_id=1, source_target_pairs={{0,8},{2,10},{4,12},{6,14},{8,0},{10,2},{12,4},{14,6},{16,24},{18,... | collective-permute-start | bytes 589832 | tf_op jit(solution)/shard_map/ppermute | solution.py:23
  354.4 14.7 %while.54 = (s32[]{:T(128)}, f32[384,3072]{1,0:T(8,128)}, f32[4,384,512]{2,1,0:T(8,128)S(1)}, f32[1024,3072]{1,0:T(8,128)}, s32[]{:T(128)}, /*index=5*/s32[]{:T(128)}, s32[]{:T(128)}, s32[]{:T(128)}) while((s32[]{:T(128)}, f32[384,3072]{1,0:T(8,128)}, f32[4,384,512]{2,1,0:T(8,128)S(1)}, f32[1024,3072]{1,0:T(8,128)}, s32[]{:T(128)}, ...), condition=%wide.region_10.11_spmd, body=%wide.region_9.10_spmd.sunk | while | flops 905969664 | bytes 3540611 | solution.py:121
  365.4 3.7 fusion.111
  388.8 12.4 %collective-permute-done.42 = f32[1,1,4,24,512]{4,2,0,3,1:T(4,128)S(1)} collective-permute-done((f32[1,1,4,24,512]{4,2,0,3,1:T(4,128)S(1)}, f32[1,1,4,24,512]{4,2,0,3,1:T(4,128)S(1)}, u32[]{:S(2)}, u32[]{:S(2)}) %collective-permute-start.42) | collective-permute-done | bytes 196640 | tf_op jit(solution)/shard_map/ppermute | solution.py:23
  401.1 3.8 collective-permute-start.47
  408.6 8.3 %collective-permute-done.44 = f32[1,1,4,24,512]{4,2,0,3,1:T(4,128)S(1)} collective-permute-done((f32[1,1,4,24,512]{4,2,0,3,1:T(4,128)S(1)}, f32[1,1,4,24,512]{4,2,0,3,1:T(4,128)S(1)}, u32[]{:S(2)}, u32[]{:S(2)}) %collective-permute-start.44) | collective-permute-done | bytes 196640 | tf_op jit(solution)/shard_map/ppermute | solution.py:23
  421.4 4.9 %collective-permute-done.49 = f32[1,1,4,24,512]{4,2,0,3,1:T(4,128)S(1)} collective-permute-done((f32[1,1,4,24,512]{4,2,0,3,1:T(4,128)S(1)}, f32[1,1,4,24,512]{4,2,0,3,1:T(4,128)S(1)}, u32[]{:S(2)}, u32[]{:S(2)}) %collective-permute-start.49) | collective-permute-done | bytes 196640 | tf_op jit(solution)/shard_map/ppermute | solution.py:23
  429.1 14.6 %while.55 = (s32[]{:T(128)}, f32[384,3072]{1,0:T(8,128)}, f32[4,384,512]{2,1,0:T(8,128)S(1)}, f32[1024,3072]{1,0:T(8,128)}, s32[]{:T(128)}, /*index=5*/s32[]{:T(128)}, s32[]{:T(128)}, s32[]{:T(128)}) while((s32[]{:T(128)}, f32[384,3072]{1,0:T(8,128)}, f32[4,384,512]{2,1,0:T(8,128)S(1)}, f32[1024,3072]{1,0:T(8,128)}, s32[]{:T(128)}, ...), condition=%wide.region_12.13_spmd, body=%wide.region_11.12_spmd.sunk | while | flops 905969664 | bytes 3540611 | solution.py:121
  443.8 7.0 %add.330 = f32[384,3072]{1,0:T(8,128)} add(f32[384,3072]{1,0:T(8,128)} %get-tuple-element.353, f32[384,3072]{1,0:T(8,128)} %get-tuple-element.354) | non-fusion elementwise | flops 1179648 | bytes 14155776 | tf_op jit(solution)/shard_map/add | solution.py:139
  453.7 17.0 %reduce-scatter.2.cloned.1.call-done = f32[192,3072]{1,0:T(8,128)} async-done(((f32[384,3072]{1,0:T(8,128)}), f32[192,3072]{1,0:T(8,128)}) %reduce-scatter.2.cloned.1.call-update) | async-done | bytes 2359312 | tf_op jit(solution)/shard_map/reduce_scatter | solution.py:141
  (257 shorter events, 198.8 us)
Async XLA Ops:
  7.3 463.4 %reduce-scatter.2.cloned.1.call-start = ((), (), s32[]{:S(2)}) async-start(), calls=%async_computation.2 | async-start | bytes 7077888 | tf_op jit(solution)/shard_map/reduce_scatter | solution.py:141
  43.2 27.9 %collective-permute-start.5 = (f32[1,1,4,24,512]{4,3,2,1,0:T(8,128)}, f32[1,1,4,24,512]{4,3,2,1,0:T(8,128)}, u32[]{:S(2)}, u32[]{:S(2)}) collective-permute-start(f32[1,1,4,24,512]{4,3,2,1,0:T(8,128)} %get-tuple-element.443), channel_id=1, source_target_pairs={{0,2},{2,0},{4,6},{6,4},{8,10},{10,8},{12,14},{14,12},{16,18},{18,... | collective-permute-start | bytes 589832 | tf_op jit(solution)/shard_map/ppermute | solution.py:23
  45.0 30.3 %collective-permute-start.6 = (f32[1,1,4,24,512]{4,3,2,1,0:T(8,128)}, f32[1,1,4,24,512]{4,3,2,1,0:T(8,128)}, u32[]{:S(2)}, u32[]{:S(2)}) collective-permute-start(f32[1,1,4,24,512]{4,3,2,1,0:T(8,128)} %get-tuple-element.442), channel_id=1, source_target_pairs={{0,4},{2,6},{4,0},{6,2},{8,12},{10,14},{12,8},{14,10},{16,20},{18,... | collective-permute-start | bytes 589832 | tf_op jit(solution)/shard_map/ppermute | solution.py:23
  46.5 30.6 %collective-permute-start.7 = (f32[1,1,4,24,512]{4,3,2,1,0:T(8,128)}, f32[1,1,4,24,512]{4,3,2,1,0:T(8,128)}, u32[]{:S(2)}, u32[]{:S(2)}) collective-permute-start(f32[1,1,4,24,512]{4,3,2,1,0:T(8,128)} %get-tuple-element.441), channel_id=1, source_target_pairs={{0,6},{2,4},{4,2},{6,0},{8,14},{10,12},{12,10},{14,8},{16,22},{18,... | collective-permute-start | bytes 589832 | tf_op jit(solution)/shard_map/ppermute | solution.py:23
  46.6 35.1 %collective-permute-start.8 = (f32[1,1,4,24,512]{4,3,2,1,0:T(8,128)}, f32[1,1,4,24,512]{4,3,2,1,0:T(8,128)}, u32[]{:S(2)}, u32[]{:S(2)}) collective-permute-start(f32[1,1,4,24,512]{4,3,2,1,0:T(8,128)} %get-tuple-element.440), channel_id=1, source_target_pairs={{0,8},{2,10},{4,12},{6,14},{8,0},{10,2},{12,4},{14,6},{16,24},{18,... | collective-permute-start | bytes 589832 | tf_op jit(solution)/shard_map/ppermute | solution.py:23
  48.5 36.3 %collective-permute-start.9 = (f32[1,1,4,24,512]{4,3,2,1,0:T(8,128)}, f32[1,1,4,24,512]{4,3,2,1,0:T(8,128)}, u32[]{:S(2)}, u32[]{:S(2)}) collective-permute-start(f32[1,1,4,24,512]{4,3,2,1,0:T(8,128)} %get-tuple-element.439), channel_id=1, source_target_pairs={{0,10},{2,8},{4,14},{6,12},{8,2},{10,0},{12,6},{14,4},{16,26},{18,... | collective-permute-start | bytes 589832 | tf_op jit(solution)/shard_map/ppermute | solution.py:23
  77.1 29.8 %collective-permute-start.12 = (f32[1,1,4,24,512]{4,3,2,1,0:T(8,128)S(1)}, f32[1,1,4,24,512]{4,3,2,1,0:T(8,128)S(1)}, u32[]{:S(2)}, u32[]{:S(2)}) collective-permute-start(f32[1,1,4,24,512]{4,3,2,1,0:T(8,128)S(1)} %copy-done.24), channel_id=1, source_target_pairs={{0,16},{2,18},{4,20},{6,22},{8,24},{10,26},{12,28},{14,30},{16,0},... | collective-permute-start | bytes 589832 | tf_op jit(solution)/shard_map/ppermute | solution.py:23
  81.8 34.7 %collective-permute-start.13 = (f32[1,1,4,24,512]{4,3,2,1,0:T(8,128)S(1)}, f32[1,1,4,24,512]{4,3,2,1,0:T(8,128)S(1)}, u32[]{:S(2)}, u32[]{:S(2)}) collective-permute-start(f32[1,1,4,24,512]{4,3,2,1,0:T(8,128)S(1)} %copy-done.22), channel_id=1, source_target_pairs={{0,18},{2,16},{4,22},{6,20},{8,26},{10,24},{12,30},{14,28},{16,2},... | collective-permute-start | bytes 589832 | tf_op jit(solution)/shard_map/ppermute | solution.py:23
  84.8 40.5 %collective-permute-start.14 = (f32[1,1,4,24,512]{4,3,2,1,0:T(8,128)S(1)}, f32[1,1,4,24,512]{4,3,2,1,0:T(8,128)S(1)}, u32[]{:S(2)}, u32[]{:S(2)}) collective-permute-start(f32[1,1,4,24,512]{4,3,2,1,0:T(8,128)S(1)} %copy-done.20), channel_id=1, source_target_pairs={{0,20},{2,22},{4,16},{6,18},{8,28},{10,30},{12,24},{14,26},{16,4},... | collective-permute-start | bytes 589832 | tf_op jit(solution)/shard_map/ppermute | solution.py:23
  90.2 41.1 %collective-permute-start.15 = (f32[1,1,4,24,512]{4,3,2,1,0:T(8,128)S(1)}, f32[1,1,4,24,512]{4,3,2,1,0:T(8,128)S(1)}, u32[]{:S(2)}, u32[]{:S(2)}) collective-permute-start(f32[1,1,4,24,512]{4,3,2,1,0:T(8,128)S(1)} %copy-done.18), channel_id=1, source_target_pairs={{0,22},{2,20},{4,18},{6,16},{8,30},{10,28},{12,26},{14,24},{16,6},... | collective-permute-start | bytes 589832 | tf_op jit(solution)/shard_map/ppermute | solution.py:23
  91.0 41.1 %collective-permute-start.16 = (f32[1,1,4,24,512]{4,3,2,1,0:T(8,128)S(1)}, f32[1,1,4,24,512]{4,3,2,1,0:T(8,128)S(1)}, u32[]{:S(2)}, u32[]{:S(2)}) collective-permute-start(f32[1,1,4,24,512]{4,3,2,1,0:T(8,128)S(1)} %copy-done.17), channel_id=1, source_target_pairs={{0,24},{2,26},{4,28},{6,30},{8,16},{10,18},{12,20},{14,22},{16,8},... | collective-permute-start | bytes 589832 | tf_op jit(solution)/shard_map/ppermute | solution.py:23
  160.8 26.1 %collective-permute-start.22 = (f32[1,2,4,24,512]{4,2,0,3,1:T(4,128)}, f32[1,2,4,24,512]{4,2,0,3,1:T(4,128)S(1)}, u32[]{:S(2)}, u32[]{:S(2)}) collective-permute-start(f32[1,2,4,24,512]{4,2,0,3,1:T(4,128)} %get-tuple-element.401), channel_id=1, source_target_pairs={{0,6},{2,4},{4,2},{6,0},{8,14},{10,12},{12,10},{14,8},{16,22},{18,... | collective-permute-start | bytes 1179656 | tf_op jit(solution)/shard_map/ppermute | solution.py:23
  162.3 42.5 %collective-permute-start.23 = (f32[1,2,4,24,512]{4,2,0,3,1:T(4,128)}, f32[1,2,4,24,512]{4,2,0,3,1:T(4,128)S(1)}, u32[]{:S(2)}, u32[]{:S(2)}) collective-permute-start(f32[1,2,4,24,512]{4,2,0,3,1:T(4,128)} %get-tuple-element.402), channel_id=1, source_target_pairs={{0,8},{2,10},{4,12},{6,14},{8,0},{10,2},{12,4},{14,6},{16,24},{18,... | collective-permute-start | bytes 1179656 | tf_op jit(solution)/shard_map/ppermute | solution.py:23
  177.1 28.6 %collective-permute-start.24 = (f32[1,2,4,24,512]{4,2,0,3,1:T(4,128)S(1)}, f32[1,2,4,24,512]{4,2,0,3,1:T(4,128)S(1)}, u32[]{:S(2)}, u32[]{:S(2)}) collective-permute-start(f32[1,2,4,24,512]{4,2,0,3,1:T(4,128)S(1)} %get-tuple-element.404), channel_id=1, source_target_pairs={{0,10},{2,8},{4,14},{6,12},{8,2},{10,0},{12,6},{14,4},{16,26},{18,... | collective-permute-start | bytes 1179656 | tf_op jit(solution)/shard_map/ppermute | solution.py:23
  177.2 38.0 %collective-permute-start.25 = (f32[1,2,4,24,512]{4,2,0,3,1:T(4,128)S(1)}, f32[1,2,4,24,512]{4,2,0,3,1:T(4,128)S(1)}, u32[]{:S(2)}, u32[]{:S(2)}) collective-permute-start(f32[1,2,4,24,512]{4,2,0,3,1:T(4,128)S(1)} %get-tuple-element.405), channel_id=1, source_target_pairs={{0,12},{2,14},{4,8},{6,10},{8,4},{10,6},{12,0},{14,2},{16,28},{18,... | collective-permute-start | bytes 1179656 | tf_op jit(solution)/shard_map/ppermute | solution.py:23
  186.8 33.9 %collective-permute-start.26 = (f32[1,2,4,24,512]{4,2,0,3,1:T(4,128)S(1)}, f32[1,2,4,24,512]{4,2,0,3,1:T(4,128)S(1)}, u32[]{:S(2)}, u32[]{:S(2)}) collective-permute-start(f32[1,2,4,24,512]{4,2,0,3,1:T(4,128)S(1)} %get-tuple-element.406), channel_id=1, source_target_pairs={{0,14},{2,12},{4,10},{6,8},{8,6},{10,4},{12,2},{14,0},{16,30},{18,... | collective-permute-start | bytes 1179656 | tf_op jit(solution)/shard_map/ppermute | solution.py:23
  187.0 77.8 %collective-permute-start.27 = (f32[1,2,4,24,512]{4,2,0,3,1:T(4,128)S(1)}, f32[1,2,4,24,512]{4,2,0,3,1:T(4,128)S(1)}, u32[]{:S(2)}, u32[]{:S(2)}) collective-permute-start(f32[1,2,4,24,512]{4,2,0,3,1:T(4,128)S(1)} %get-tuple-element.407), channel_id=1, source_target_pairs={{0,16},{2,18},{4,20},{6,22},{8,24},{10,26},{12,28},{14,30},{16,0},... | collective-permute-start | bytes 1179656 | tf_op jit(solution)/shard_map/ppermute | solution.py:23
  204.8 73.9 %collective-permute-start.28 = (f32[1,2,4,24,512]{4,2,0,3,1:T(4,128)S(1)}, f32[1,2,4,24,512]{4,2,0,3,1:T(4,128)S(1)}, u32[]{:S(2)}, u32[]{:S(2)}) collective-permute-start(f32[1,2,4,24,512]{4,2,0,3,1:T(4,128)S(1)} %get-tuple-element.408), channel_id=1, source_target_pairs={{0,18},{2,16},{4,22},{6,20},{8,26},{10,24},{12,30},{14,28},{16,2},... | collective-permute-start | bytes 1179656 | tf_op jit(solution)/shard_map/ppermute | solution.py:23
  205.7 88.3 %collective-permute-start.29 = (f32[1,2,4,24,512]{4,2,0,3,1:T(4,128)S(1)}, f32[1,2,4,24,512]{4,2,0,3,1:T(4,128)S(1)}, u32[]{:S(2)}, u32[]{:S(2)}) collective-permute-start(f32[1,2,4,24,512]{4,2,0,3,1:T(4,128)S(1)} %get-tuple-element.410), channel_id=1, source_target_pairs={{0,20},{2,22},{4,16},{6,18},{8,28},{10,30},{12,24},{14,26},{16,4},... | collective-permute-start | bytes 1179656 | tf_op jit(solution)/shard_map/ppermute | solution.py:23
  215.2 85.3 %collective-permute-start.30 = (f32[1,2,4,24,512]{4,2,0,3,1:T(4,128)S(1)}, f32[1,2,4,24,512]{4,2,0,3,1:T(4,128)S(1)}, u32[]{:S(2)}, u32[]{:S(2)}) collective-permute-start(f32[1,2,4,24,512]{4,2,0,3,1:T(4,128)S(1)} %get-tuple-element.411), channel_id=1, source_target_pairs={{0,22},{2,20},{4,18},{6,16},{8,30},{10,28},{12,26},{14,24},{16,6},... | collective-permute-start | bytes 1179656 | tf_op jit(solution)/shard_map/ppermute | solution.py:23
  220.7 79.8 %collective-permute-start.31 = (f32[1,2,4,24,512]{4,2,0,3,1:T(4,128)S(1)}, f32[1,2,4,24,512]{4,2,0,3,1:T(4,128)S(1)}, u32[]{:S(2)}, u32[]{:S(2)}) collective-permute-start(f32[1,2,4,24,512]{4,2,0,3,1:T(4,128)S(1)} %get-tuple-element.412), channel_id=1, source_target_pairs={{0,24},{2,26},{4,28},{6,30},{8,16},{10,18},{12,20},{14,22},{16,8},... | collective-permute-start | bytes 1179656 | tf_op jit(solution)/shard_map/ppermute | solution.py:23
  264.8 35.9 %collective-permute-start.32 = (f32[1,2,4,24,512]{4,2,0,3,1:T(4,128)S(1)}, f32[1,2,4,24,512]{4,2,0,3,1:T(4,128)S(1)}, u32[]{:S(2)}, u32[]{:S(2)}) collective-permute-start(f32[1,2,4,24,512]{4,2,0,3,1:T(4,128)S(1)} %get-tuple-element.409), channel_id=1, source_target_pairs={{0,26},{2,24},{4,30},{6,28},{8,18},{10,16},{12,22},{14,20},{16,10}... | collective-permute-start | bytes 1179656 | tf_op jit(solution)/shard_map/ppermute | solution.py:23
  322.2 47.4 %collective-permute-start.35 = (f32[1,1,4,24,512]{4,2,0,3,1:T(4,128)}, f32[1,1,4,24,512]{4,2,0,3,1:T(4,128)}, u32[]{:S(2)}, u32[]{:S(2)}) collective-permute-start(f32[1,1,4,24,512]{4,2,0,3,1:T(4,128)} %get-tuple-element.427), channel_id=1, source_target_pairs={{0,2},{2,0},{4,6},{6,4},{8,10},{10,8},{12,14},{14,12},{16,18},{18,... | collective-permute-start | bytes 589832 | tf_op jit(solution)/shard_map/ppermute | solution.py:23
  325.1 47.4 %collective-permute-start.36 = (f32[1,1,4,24,512]{4,2,0,3,1:T(4,128)}, f32[1,1,4,24,512]{4,2,0,3,1:T(4,128)}, u32[]{:S(2)}, u32[]{:S(2)}) collective-permute-start(f32[1,1,4,24,512]{4,2,0,3,1:T(4,128)} %get-tuple-element.426), channel_id=1, source_target_pairs={{0,4},{2,6},{4,0},{6,2},{8,12},{10,14},{12,8},{14,10},{16,20},{18,... | collective-permute-start | bytes 589832 | tf_op jit(solution)/shard_map/ppermute | solution.py:23
  325.1 49.9 %collective-permute-start.37 = (f32[1,1,4,24,512]{4,2,0,3,1:T(4,128)}, f32[1,1,4,24,512]{4,2,0,3,1:T(4,128)}, u32[]{:S(2)}, u32[]{:S(2)}) collective-permute-start(f32[1,1,4,24,512]{4,2,0,3,1:T(4,128)} %get-tuple-element.425), channel_id=1, source_target_pairs={{0,6},{2,4},{4,2},{6,0},{8,14},{10,12},{12,10},{14,8},{16,22},{18,... | collective-permute-start | bytes 589832 | tf_op jit(solution)/shard_map/ppermute | solution.py:23
  326.6 52.0 %collective-permute-start.38 = (f32[1,1,4,24,512]{4,2,0,3,1:T(4,128)}, f32[1,1,4,24,512]{4,2,0,3,1:T(4,128)}, u32[]{:S(2)}, u32[]{:S(2)}) collective-permute-start(f32[1,1,4,24,512]{4,2,0,3,1:T(4,128)} %get-tuple-element.424), channel_id=1, source_target_pairs={{0,8},{2,10},{4,12},{6,14},{8,0},{10,2},{12,4},{14,6},{16,24},{18,... | collective-permute-start | bytes 589832 | tf_op jit(solution)/shard_map/ppermute | solution.py:23
  348.7 32.3 %collective-permute-start.39 = (f32[1,1,4,24,512]{4,2,0,3,1:T(4,128)}, f32[1,1,4,24,512]{4,2,0,3,1:T(4,128)}, u32[]{:S(2)}, u32[]{:S(2)}) collective-permute-start(f32[1,1,4,24,512]{4,2,0,3,1:T(4,128)} %get-tuple-element.423), channel_id=1, source_target_pairs={{0,10},{2,8},{4,14},{6,12},{8,2},{10,0},{12,6},{14,4},{16,26},{18,... | collective-permute-start | bytes 589832 | tf_op jit(solution)/shard_map/ppermute | solution.py:23
  375.0 26.1 %collective-permute-start.42 = (f32[1,1,4,24,512]{4,2,0,3,1:T(4,128)S(1)}, f32[1,1,4,24,512]{4,2,0,3,1:T(4,128)S(1)}, u32[]{:S(2)}, u32[]{:S(2)}) collective-permute-start(f32[1,1,4,24,512]{4,2,0,3,1:T(4,128)S(1)} %copy-done.23), channel_id=1, source_target_pairs={{0,16},{2,18},{4,20},{6,22},{8,24},{10,26},{12,28},{14,30},{16,0},... | collective-permute-start | bytes 589832 | tf_op jit(solution)/shard_map/ppermute | solution.py:23
  378.7 26.9 %collective-permute-start.43 = (f32[1,1,4,24,512]{4,2,0,3,1:T(4,128)S(1)}, f32[1,1,4,24,512]{4,2,0,3,1:T(4,128)S(1)}, u32[]{:S(2)}, u32[]{:S(2)}) collective-permute-start(f32[1,1,4,24,512]{4,2,0,3,1:T(4,128)S(1)} %copy-done.21), channel_id=1, source_target_pairs={{0,18},{2,16},{4,22},{6,20},{8,26},{10,24},{12,30},{14,28},{16,2},... | collective-permute-start | bytes 589832 | tf_op jit(solution)/shard_map/ppermute | solution.py:23
  381.0 35.9 %collective-permute-start.44 = (f32[1,1,4,24,512]{4,2,0,3,1:T(4,128)S(1)}, f32[1,1,4,24,512]{4,2,0,3,1:T(4,128)S(1)}, u32[]{:S(2)}, u32[]{:S(2)}) collective-permute-start(f32[1,1,4,24,512]{4,2,0,3,1:T(4,128)S(1)} %copy-done.19), channel_id=1, source_target_pairs={{0,20},{2,22},{4,16},{6,18},{8,28},{10,30},{12,24},{14,26},{16,4},... | collective-permute-start | bytes 589832 | tf_op jit(solution)/shard_map/ppermute | solution.py:23
  384.7 36.3 %collective-permute-start.45 = (f32[1,1,4,24,512]{4,2,0,3,1:T(4,128)S(1)}, f32[1,1,4,24,512]{4,2,0,3,1:T(4,128)S(1)}, u32[]{:S(2)}, u32[]{:S(2)}) collective-permute-start(f32[1,1,4,24,512]{4,2,0,3,1:T(4,128)S(1)} %copy-done.16), channel_id=1, source_target_pairs={{0,22},{2,20},{4,18},{6,16},{8,30},{10,28},{12,26},{14,24},{16,6},... | collective-permute-start | bytes 589832 | tf_op jit(solution)/shard_map/ppermute | solution.py:23
  386.3 34.8 %collective-permute-start.46 = (f32[1,1,4,24,512]{4,2,0,3,1:T(4,128)S(1)}, f32[1,1,4,24,512]{4,2,0,3,1:T(4,128)S(1)}, u32[]{:S(2)}, u32[]{:S(2)}) collective-permute-start(f32[1,1,4,24,512]{4,2,0,3,1:T(4,128)S(1)} %copy-done.14), channel_id=1, source_target_pairs={{0,24},{2,26},{4,28},{6,30},{8,16},{10,18},{12,20},{14,22},{16,8},... | collective-permute-start | bytes 589832 | tf_op jit(solution)/shard_map/ppermute | solution.py:23
  (51 other events, 855.0 us)
Sparse Core Ops, SparseCore 0:
  8.9 17.1 all-gather.1
  450.9 19.7 reduce-scatter.1
